TPU v7x, 512 devices: a whole 4x8x8 slice. The times are simulated.
512 devices in a mesh: section: 4 (over z_hi, core), seq: 32 (over x, y), head: 4 (over z_lo).
Axes of the slice: x: 4, y: 8, z: 8 (z_hi: 2, z_lo: 4; z = z_hi * 4 + z_lo), core: 2. Of those that a mesh axis runs over, the one named last changes fastest.
Arguments:
- query_heads: bfloat16 [4, 6144, 3072], P('section', 'seq', 'head'), may hold values from -6 to 6
- key_heads: bfloat16 [4, 6144, 3072], P('section', 'seq', 'head'), may hold values from -6 to 6
- value_heads: bfloat16 [4, 6144, 3072], P('section', 'seq', 'head'), may hold values from -6 to 6
- stream: bfloat16 [4, 6144, 3072], P('section', 'seq', 'head'), may hold values from -1.5 to 1.5
- out_weight: bfloat16 [4, 3072, 3072], P('section', 'head', 'seq'), may hold values from -0.109375 to 0.109375
- gate_scale: float32 [4, 3072], P('section', 'head'), may hold values from 0.5 to 1.5
- windows: int32 [16, 27], replicated, may hold values from -1 to 15, as said below
Outputs:
- handed: bfloat16 [4, 6144, 3072], P('section', 'seq', 'head')
Inputs may be any that keep to these rules, and one draw needn't show every extreme that they name: `windows`: row t lists, in an order drawn for each row, tile t + dt for every dt in -1, 0, 1 with 0 <= t + dt < 16 and tile t + dt in the same clip as t, and -1 in all its other slots; clips are runs of whole consecutive temporal tiles.
All inputs are finite; a program needn't handle non-finite values.
Results may differ from a plain program's by a relative error of at most 0.012.
Values may be sent and summed in bfloat16 or wider, within the bound.
No kernel may reach another device: no remote copies, remote signals or barrier semaphores. Data moves between devices by JAX's collectives and lax.ppermute only.
A program may use at most 64 MiB of HBM per device.

v0:
```python
from functools import partial
import math
import jax
import jax.numpy as jnp
from jax import lax
from jax.sharding import Mesh, PartitionSpec as P

HD = 128
SPATIAL = 1


def shifted(block, axis, count, distance, wanted):
    devices = range(count)
    route = [(i - distance, i) for i in devices if i - distance in devices and wanted(i)]
    return lax.ppermute(block, axis, route)


def needs(offset):
    if offset == 3:
        return lambda i: i % 2 == 1
    if offset == -3:
        return lambda i: i % 2 == 0
    return lambda i: True


def linear_pairs(sizes, mapping):

    def flat(index):
        value = 0
        for part, size in zip(index, sizes):
            value = value * size + part
        return value

    grid = [[]]
    for size in sizes:
        grid = [index + [part] for index in grid for part in range(size)]
    return [(flat(index), flat(mapping(*index))) for index in grid]


def from_behind(value, axis, steps):
    count = lax.axis_size(axis)
    pairs = [(source, (source + steps) % count) for source in range(count)]
    return lax.ppermute(value, axis, pairs)


def split_heads(slab, head_count):
    return slab.reshape(slab.shape[0], head_count, slab.shape[1] // head_count)


def tile_maxima(key_slab, head_count, spatial_count):
    parts = split_heads(key_slab, head_count).astype(jnp.float32)
    lengths = jnp.sqrt(jnp.sum(parts * parts, axis=2))
    return jnp.max(lengths.reshape(spatial_count, -1, head_count), axis=1)


def slab_keep(nearby, slab_tile, in_range, spatial_count, temporal_count):
    first = jnp.clip(slab_tile, 0, temporal_count - 1) * spatial_count
    return lax.dynamic_slice_in_dim(nearby, first, spatial_count, 1) & in_range


def attend(
    running,
    slab_entry,
    keep,
    query_parts,
    row_bound,
    head_count,
    spatial_count,
    tile_rows,
    score_scale,
):
    weighted, summed = running
    row_count = query_parts.shape[0]
    slab_keys = split_heads(slab_entry[0], head_count)
    slab_values = split_heads(slab_entry[1], head_count)
    scores = (
        jnp.einsum("qhd,khd->hqk", query_parts, slab_keys, preferred_element_type=jnp.float32)
        * score_scale
    )
    row_keep = jnp.broadcast_to(
        keep[:, None, :, None], (spatial_count, tile_rows, spatial_count, tile_rows)
    )
    row_keep = row_keep.reshape(row_count, row_count)
    weights = jnp.where(row_keep[None], jnp.exp(scores - row_bound.T[:, :, None]), 0.0)
    summed = summed + jnp.sum(weights, axis=2)
    weighted = weighted + jnp.einsum(
        "hqk,khd->qhd",
        weights.astype(jnp.bfloat16),
        slab_values,
        preferred_element_type=jnp.float32,
    )
    return (weighted, summed)


def on_device(query_heads, key_heads, value_heads, stream, out_weight, gate_scale, windows):
    queries = query_heads[0]
    own_keys = key_heads[0]
    own_values = value_heads[0]
    row_count, feature_count = queries.shape
    head_count = feature_count // HD
    spatial_count = SPATIAL
    tile_rows = row_count // spatial_count
    tile_count = windows.shape[0]
    temporal_count = tile_count // spatial_count
    score_scale = 1.0 / math.sqrt(HD)
    x_count = lax.axis_size("sx")
    y_count = lax.axis_size("sy")
    head_groups = lax.axis_size("head")
    sections = lax.axis_size("section")
    seq_count = x_count * y_count
    x_index = lax.axis_index("sx")
    y_index = lax.axis_index("sy")
    position = x_index * y_count + y_index
    parity = position % 2
    temporal = position // 2
    allowed = jnp.any(
        windows[:, :, None] == jnp.arange(tile_count, dtype=jnp.int32)[None, None, :], axis=1
    )
    row_allowed = lax.dynamic_index_in_dim(allowed, temporal, 0, keepdims=False)
    seq = ("sx", "sy")
    half = feature_count // 2
    own_heads = head_count // 2
    tile_len = 2 * row_count
    partner = [(i, i ^ 1) for i in range(seq_count)]

    def partner_half(block):
        return lax.dynamic_slice_in_dim(block, (1 - parity) * half, half, 1)

    def own_half(block):
        return lax.dynamic_slice_in_dim(block, parity * half, half, 1)

    sent = lax.ppermute(
        (partner_half(queries), partner_half(own_keys), partner_half(own_values)), seq, partner
    )

    def whole_tile(mine, theirs):
        return jnp.where(
            parity == 0,
            jnp.concatenate([mine, theirs], axis=0),
            jnp.concatenate([theirs, mine], axis=0),
        )

    tile_q = whole_tile(own_half(queries), sent[0])
    tile_k = whole_tile(own_half(own_keys), sent[1])
    tile_v = whole_tile(own_half(own_values), sent[2])
    before = lax.ppermute((tile_k, tile_v), seq, [(i, i + 2) for i in range(seq_count - 2)])
    after = lax.ppermute((tile_k, tile_v), seq, [(i, i - 2) for i in range(2, seq_count)])
    key_tiles = [before, (tile_k, tile_v), after]
    keeps = []
    for step in (-1, 0, 1):
        near = temporal + step
        in_range = (near >= 0) & (near < temporal_count)
        listed = lax.dynamic_index_in_dim(
            row_allowed, jnp.clip(near, 0, temporal_count - 1), 0, keepdims=False
        )
        keeps.append(in_range & listed)
    bound = jnp.zeros((own_heads,), jnp.float32)
    for (keys, _), keep in zip(key_tiles, keeps):
        key_float = keys.reshape(tile_len, own_heads, HD).astype(jnp.float32)
        key_lengths = jnp.sqrt(jnp.sum(key_float * key_float, axis=2))
        bound = jnp.maximum(bound, jnp.where(keep, jnp.max(key_lengths, axis=0), 0.0))
    query_parts = tile_q.reshape(tile_len, own_heads, HD)
    query_float = query_parts.astype(jnp.float32)
    query_lengths = jnp.sqrt(jnp.sum(query_float * query_float, axis=2))
    row_bound = query_lengths * bound[None, :] * score_scale
    weight_block = lax.all_gather(out_weight[0], "sy", axis=1, tiled=True)
    swap = linear_pairs((x_count, head_groups), lambda a, b: (b, a))
    stream_in, gate_in, _ = lax.optimization_barrier((stream[0], gate_scale[0], tile_k))
    stream_block = lax.ppermute(stream_in, ("sx", "head"), swap)
    gate_block = lax.ppermute(gate_in, ("sx", "head"), swap)
    weight_block, row_bound, stream_block, gate_block = lax.optimization_barrier(
        (weight_block, row_bound, stream_block, gate_block)
    )
    weighted = jnp.zeros((tile_len, own_heads, HD), jnp.float32)
    summed = jnp.zeros((own_heads, tile_len), jnp.float32)
    for (keys, values), keep in zip(key_tiles, keeps):
        key_parts = keys.reshape(tile_len, own_heads, HD)
        value_parts = values.reshape(tile_len, own_heads, HD)
        scores = (
            jnp.einsum("qhd,khd->hqk", query_parts, key_parts, preferred_element_type=jnp.float32)
            * score_scale
        )
        weights = jnp.where(keep, jnp.exp(scores - row_bound.T[:, :, None]), 0.0)
        summed = summed + jnp.sum(weights, axis=2)
        weighted = weighted + jnp.einsum(
            "hqk,khd->qhd",
            weights.astype(jnp.bfloat16),
            value_parts,
            preferred_element_type=jnp.float32,
        )
    tile_out = (weighted / summed.T[:, :, None]).astype(jnp.bfloat16).reshape(tile_len, half)
    mine_rows = lax.dynamic_slice_in_dim(tile_out, parity * row_count, row_count, 0)
    their_rows = lax.dynamic_slice_in_dim(tile_out, (1 - parity) * row_count, row_count, 0)
    back = lax.ppermute(their_rows, seq, partner)
    attended = jnp.where(
        parity == 0,
        jnp.concatenate([mine_rows, back], axis=1),
        jnp.concatenate([back, mine_rows], axis=1),
    )
    spread = jnp.broadcast_to(attended[None], (x_count,) + attended.shape)
    token_parts = lax.all_to_all(spread, "sx", 0, 0)
    group_index = lax.axis_index("head")

    def term_for(slab_x):
        part = lax.dynamic_index_in_dim(token_parts, slab_x, 0, keepdims=False)
        return jnp.dot(part, weight_block, preferred_element_type=jnp.float32).astype(jnp.bfloat16)

    received = []
    for shift in range(1, head_groups):
        outgoing = term_for((group_index + shift) % head_groups)
        route = [(g, (g + shift) % head_groups) for g in range(head_groups)]
        received.append(lax.ppermute(outgoing, "head", route))
    mixed = term_for(group_index).astype(jnp.float32)
    for term in received:
        mixed = mixed + term.astype(jnp.float32)
    updated = (stream_block.astype(jnp.float32) + gate_block[None, :] * mixed).astype(jnp.bfloat16)
    hand = linear_pairs(
        (sections, x_count, head_groups), lambda s, a, b: ((s + 1) % sections, b, a)
    )
    handed = lax.ppermute(updated, ("section", "sx", "head"), hand)
    return handed[None]


def solution(mesh):
    sections, seq_count, head_count = mesh.devices.shape
    x_count = 4 if seq_count % 4 == 0 else 1
    split_mesh = Mesh(
        mesh.devices.reshape(sections, x_count, seq_count // x_count, head_count),
        ("section", "sx", "sy", "head"),
    )
    seq = ("sx", "sy")
    in_specs = (
        P("section", seq, "head"),
        P("section", seq, "head"),
        P("section", seq, "head"),
        P("section", seq, "head"),
        P("section", "head", seq),
        P("section", "head"),
        P(),
    )
    out_specs = P("section", seq, "head")
    return jax.shard_map(
        on_device, mesh=split_mesh, in_specs=in_specs, out_specs=out_specs, check_vma=False
    )
```

profile of v0, /device:TPU:153, one launch (start us, length us, event | category | flops | bytes accessed | tf_op | source)
XLA Modules:
  0.0 161.0 jit_solution(1921376385303755416)
XLA Ops:
  7.3 1.0 dynamic-slice_bitcast_fusion.2
  8.3 2.1 %collective-permute-start = (bf16[192,384]{1,0:T(8,128)(2,1)S(1)}, bf16[192,384]{1,0:T(8,128)(2,1)S(1)}, u32[]{:S(2)}, u32[]{:S(2)}) collective-permute-start(bf16[192,384]{1,0:T(8,128)(2,1)S(1)} %get-tuple-element.27), channel_id=1, source_target_pairs={{0,4},{4,0},{8,12},{12,8},{16,20},{20,16},{24,28},{28,24},{32,36},... | collective-permute-start | bytes 442376 | tf_op jit(solution)/shard_map/ppermute | solution.py:132
  10.4 1.0 constant_dynamic-slice_fusion.3
  11.4 3.2 %collective-permute-start.1 = (bf16[192,384]{1,0:T(8,128)(2,1)S(1)}, bf16[192,384]{1,0:T(8,128)(2,1)S(1)}, u32[]{:S(2)}, u32[]{:S(2)}) collective-permute-start(bf16[192,384]{1,0:T(8,128)(2,1)S(1)} %get-tuple-element.26), channel_id=1, source_target_pairs={{0,4},{4,0},{8,12},{12,8},{16,20},{20,16},{24,28},{28,24},{32,36},... | collective-permute-start | bytes 442376 | tf_op jit(solution)/shard_map/ppermute | solution.py:132
  14.7 2.1 %collective-permute-start.6 = (bf16[192,384]{1,0:T(8,128)(2,1)S(1)}, bf16[192,384]{1,0:T(8,128)(2,1)S(1)}, u32[]{:S(2)}, u32[]{:S(2)}) collective-permute-start(bf16[192,384]{1,0:T(8,128)(2,1)S(1)} %get-tuple-element.24), channel_id=1, source_target_pairs={{0,4},{4,0},{8,12},{12,8},{16,20},{20,16},{24,28},{28,24},{32,36},... | collective-permute-start | bytes 442376 | tf_op jit(solution)/shard_map/ppermute | solution.py:132
  20.0 0.8 maximum_select_fusion.4
  20.8 5.4 %collective-permute-start.2 = (bf16[384,384]{1,0:T(8,128)(2,1)}, bf16[384,384]{1,0:T(8,128)(2,1)}, u32[]{:S(2)}, u32[]{:S(2)}) collective-permute-start(bf16[384,384]{1,0:T(8,128)(2,1)} %maximum_select_fusion.4), channel_id=1, source_target_pairs={{0,8},{4,12},{8,16},{12,20},{16,24},{20,28},{24,32},{28,36},{32,40... | collective-permute-start | bytes 884744 | tf_op jit(solution)/shard_map/ppermute | solution.py:146
  26.2 1.9 %collective-permute-start.3 = (bf16[384,384]{1,0:T(8,128)(2,1)}, bf16[384,384]{1,0:T(8,128)(2,1)S(1)}, u32[]{:S(2)}, u32[]{:S(2)}) collective-permute-start(bf16[384,384]{1,0:T(8,128)(2,1)} %maximum_select_fusion.4), channel_id=1, source_target_pairs={{8,0},{12,4},{16,8},{20,12},{24,16},{28,20},{32,24},{36,28},{40,32... | collective-permute-start | bytes 884744 | tf_op jit(solution)/shard_map/ppermute | solution.py:147
  29.0 1.9 %collective-permute-start.8 = (bf16[384,384]{1,0:T(8,128)(2,1)}, bf16[384,384]{1,0:T(8,128)(2,1)S(1)}, u32[]{:S(2)}, u32[]{:S(2)}) collective-permute-start(bf16[384,384]{1,0:T(8,128)(2,1)} %maximum_select_fusion.5), channel_id=1, source_target_pairs={{8,0},{12,4},{16,8},{20,12},{24,16},{28,20},{32,24},{36,28},{40,32... | collective-permute-start | bytes 884744 | tf_op jit(solution)/shard_map/ppermute | solution.py:147
  30.9 5.5 %collective-permute-start.7 = (bf16[384,384]{1,0:T(8,128)(2,1)}, bf16[384,384]{1,0:T(8,128)(2,1)S(1)}, u32[]{:S(2)}, u32[]{:S(2)}) collective-permute-start(bf16[384,384]{1,0:T(8,128)(2,1)} %maximum_select_fusion.5), channel_id=1, source_target_pairs={{0,8},{4,12},{8,16},{12,20},{16,24},{20,28},{24,32},{28,36},{32,40... | collective-permute-start | bytes 884744 | tf_op jit(solution)/shard_map/ppermute | solution.py:146
  37.1 2.8 %collective-permute-start.4 = (bf16[192,768]{1,0:T(8,128)(2,1)}, bf16[192,768]{1,0:T(8,128)(2,1)S(1)}, u32[]{:S(2)}, u32[]{:S(2)}) collective-permute-start(bf16[192,768]{1,0:T(8,128)(2,1)} %bitcast.68), channel_id=1, source_target_pairs={{0,0},{1,32},{2,64},{3,96},{32,1},{33,33},{34,65},{35,97},{64,2},{... | collective-permute-start | bytes 884744 | tf_op jit(solution)/shard_map/ppermute | solution.py:169
  41.0 3.3 %collective-permute-done.2 = bf16[384,384]{1,0:T(8,128)(2,1)} collective-permute-done((bf16[384,384]{1,0:T(8,128)(2,1)}, bf16[384,384]{1,0:T(8,128)(2,1)}, u32[]{:S(2)}, u32[]{:S(2)}) %collective-permute-start.2) | collective-permute-done | bytes 294944 | tf_op jit(solution)/shard_map/ppermute | solution.py:146
  44.3 2.4 %collective-permute-start.5 = (f32[768]{0:T(1024)S(1)}, f32[768]{0:T(1024)S(1)}, u32[]{:S(2)}, u32[]{:S(2)}) collective-permute-start(f32[768]{0:T(1024)S(1)} %reduce), channel_id=1, source_target_pairs={{0,0},{1,32},{2,64},{3,96},{32,1},{33,33},{34,65},{35,97},{64,2},{... | collective-permute-start | bytes 9224 | tf_op jit(solution)/shard_map/ppermute | solution.py:170
  46.8 1.2 copy.77
  48.7 5.0 %collective-permute-done.8 = bf16[384,384]{1,0:T(8,128)(2,1)S(1)} collective-permute-done((bf16[384,384]{1,0:T(8,128)(2,1)}, bf16[384,384]{1,0:T(8,128)(2,1)S(1)}, u32[]{:S(2)}, u32[]{:S(2)}) %collective-permute-start.8) | collective-permute-done | bytes 294944 | tf_op jit(solution)/shard_map/ppermute | solution.py:147
  53.9 6.1 %collective-permute-done.7 = bf16[384,384]{1,0:T(8,128)(2,1)S(1)} collective-permute-done((bf16[384,384]{1,0:T(8,128)(2,1)}, bf16[384,384]{1,0:T(8,128)(2,1)S(1)}, u32[]{:S(2)}, u32[]{:S(2)}) %collective-permute-start.7) | collective-permute-done | bytes 294944 | tf_op jit(solution)/shard_map/ppermute | solution.py:146
  60.3 7.2 %all-gather.3.cloned.1.call-done = bf16[1,768,768]{1,2,0:T(8,128)(2,1)} async-done(((bf16[1,768,96]{1,2,0:T(8,128)(2,1)}), bf16[1,768,768]{1,2,0:T(8,128)(2,1)}) %all-gather.3.cloned.1.call-update) | async-done | bytes 1179664 | tf_op jit(solution)/shard_map/all_gather | solution.py:166
  70.8 1.9 %collective-permute-start.9 = (bf16[192,384]{0,1:T(8,128)(2,1)S(1)}, bf16[192,384]{0,1:T(8,128)(2,1)S(1)}, u32[]{:S(2)}, u32[]{:S(2)}) collective-permute-start(bf16[192,384]{0,1:T(8,128)(2,1)S(1)} %get-tuple-element.22), channel_id=1, source_target_pairs={{0,4},{4,0},{8,12},{12,8},{16,20},{20,16},{24,28},{28,24},{32,36},... | collective-permute-start | bytes 442376 | tf_op jit(solution)/shard_map/ppermute | solution.py:194
  72.8 5.2 %collective-permute-done.9 = bf16[192,384]{0,1:T(8,128)(2,1)S(1)} collective-permute-done((bf16[192,384]{0,1:T(8,128)(2,1)S(1)}, bf16[192,384]{0,1:T(8,128)(2,1)S(1)}, u32[]{:S(2)}, u32[]{:S(2)}) %collective-permute-start.9) | collective-permute-done | bytes 147488 | tf_op jit(solution)/shard_map/ppermute | solution.py:194
  78.3 1.1 broadcast_in_dim.31
  79.4 3.9 %all-to-all-start = ((bf16[4,192,768]{2,1,0:T(8,128)(2,1)}), bf16[4,192,768]{2,1,0:T(8,128)(2,1)S(1)}, u32[]{:S(2)}, u32[]{:S(2)}) async-start(bf16[4,192,768]{2,1,0:T(8,128)(2,1)} %broadcast_in_dim.31), calls=%async_computation | async-start | bytes 2359296 | tf_op jit(solution)/shard_map/all_to_all | solution.py:201
  83.3 14.5 %all-to-all-done = bf16[4,192,768]{2,1,0:T(8,128)(2,1)S(1)} async-done(((bf16[4,192,768]{2,1,0:T(8,128)(2,1)}), bf16[4,192,768]{2,1,0:T(8,128)(2,1)S(1)}, u32[]{:S(2)}, u32[]{:S(2)}) %all-to-all-start) | async-done | bytes 1179680 | tf_op jit(solution)/shard_map/all_to_all | solution.py:201
  97.8 1.3 convolution_convert_fusion
  99.1 1.9 %collective-permute-start.12 = (bf16[192,768]{1,0:T(8,128)(2,1)}, bf16[192,768]{1,0:T(8,128)(2,1)S(1)}, u32[]{:S(2)}, u32[]{:S(2)}) collective-permute-start(bf16[192,768]{1,0:T(8,128)(2,1)} %convolution_convert_fusion), channel_id=1, source_target_pairs={{0,3},{1,0},{2,1},{3,2},{4,7},{5,4},{6,5},{7,6},{8,11},{9,8},{10,9... | collective-permute-start | bytes 884744 | tf_op jit(solution)/shard_map/ppermute | solution.py:212
  101.0 1.3 convolution_convert_fusion.1
  102.3 6.2 %collective-permute-start.11 = (bf16[192,768]{1,0:T(8,128)(2,1)}, bf16[192,768]{1,0:T(8,128)(2,1)S(1)}, u32[]{:S(2)}, u32[]{:S(2)}) collective-permute-start(bf16[192,768]{1,0:T(8,128)(2,1)} %convolution_convert_fusion.1), channel_id=1, source_target_pairs={{0,2},{1,3},{2,0},{3,1},{4,6},{5,7},{6,4},{7,5},{8,10},{9,11},{10,... | collective-permute-start | bytes 884744 | tf_op jit(solution)/shard_map/ppermute | solution.py:212
  108.4 1.3 convolution_convert_fusion.2
  109.7 1.9 %collective-permute-start.10 = (bf16[192,768]{1,0:T(8,128)(2,1)}, bf16[192,768]{1,0:T(8,128)(2,1)S(1)}, u32[]{:S(2)}, u32[]{:S(2)}) collective-permute-start(bf16[192,768]{1,0:T(8,128)(2,1)} %convolution_convert_fusion.2), channel_id=1, source_target_pairs={{0,1},{1,2},{2,3},{3,0},{4,5},{5,6},{6,7},{7,4},{8,9},{9,10},{10,1... | collective-permute-start | bytes 884744 | tf_op jit(solution)/shard_map/ppermute | solution.py:212
  111.6 13.7 %collective-permute-done.11 = bf16[192,768]{1,0:T(8,128)(2,1)S(1)} collective-permute-done((bf16[192,768]{1,0:T(8,128)(2,1)}, bf16[192,768]{1,0:T(8,128)(2,1)S(1)}, u32[]{:S(2)}, u32[]{:S(2)}) %collective-permute-start.11) | collective-permute-done | bytes 294944 | tf_op jit(solution)/shard_map/ppermute | solution.py:212
  125.3 6.6 %collective-permute-done.10 = bf16[192,768]{1,0:T(8,128)(2,1)S(1)} collective-permute-done((bf16[192,768]{1,0:T(8,128)(2,1)}, bf16[192,768]{1,0:T(8,128)(2,1)S(1)}, u32[]{:S(2)}, u32[]{:S(2)}) %collective-permute-start.10) | collective-permute-done | bytes 294944 | tf_op jit(solution)/shard_map/ppermute | solution.py:212
  132.5 3.1 %collective-permute-start.13 = (bf16[192,768]{1,0:T(8,128)(2,1)S(1)}, bf16[192,768]{1,0:T(8,128)(2,1)S(1)}, u32[]{:S(2)}, u32[]{:S(2)}) collective-permute-start(bf16[192,768]{1,0:T(8,128)(2,1)S(1)} %add_convert_fusion), channel_id=1, source_target_pairs={{0,128},{1,160},{2,192},{3,224},{32,129},{33,161},{34,193},{35,225... | collective-permute-start | bytes 884744 | tf_op jit(solution)/shard_map/ppermute | solution.py:220
  135.5 17.9 %collective-permute-done.13 = bf16[192,768]{1,0:T(8,128)(2,1)S(1)} collective-permute-done((bf16[192,768]{1,0:T(8,128)(2,1)S(1)}, bf16[192,768]{1,0:T(8,128)(2,1)S(1)}, u32[]{:S(2)}, u32[]{:S(2)}) %collective-permute-start.13) | collective-permute-done | bytes 294944 | tf_op jit(solution)/shard_map/ppermute | solution.py:220
  (54 shorter events, 10.5 us)
Async XLA Ops:
  6.5 8.1 %copy-start.1 = (bf16[1,192,768]{2,1,0:T(8,128)(2,1)S(1)}, bf16[1,192,768]{2,1,0:T(8,128)(2,1)}, u32[]{:S(2)}) copy-start(bf16[1,192,768]{2,1,0:T(8,128)(2,1)} %param.9) | copy-start | bytes 884740
  6.5 10.3 %copy-start.2 = (s32[16,27]{1,0:T(8,128)S(1)}, s32[16,27]{1,0:T(8,128)}, u32[]{:S(2)}) copy-start(s32[16,27]{1,0:T(8,128)} %param.13) | copy-start | bytes 5188
  6.5 61.0 %all-gather.3.cloned.1.call-start = ((), (), s32[]{:S(2)}) async-start(), calls=%async_computation.1 | async-start | bytes 1327104 | tf_op jit(solution)/shard_map/all_gather | solution.py:166
  8.3 11.6 %copy-start.3 = (f32[1,768]{1,0:T(1,128)S(1)}, f32[1,768]{1,0:T(1,128)}, u32[]{:S(2)}) copy-start(f32[1,768]{1,0:T(1,128)} %param.12) | copy-start | bytes 9220
  8.3 28.8 %collective-permute-start = (bf16[192,384]{1,0:T(8,128)(2,1)S(1)}, bf16[192,384]{1,0:T(8,128)(2,1)S(1)}, u32[]{:S(2)}, u32[]{:S(2)}) collective-permute-start(bf16[192,384]{1,0:T(8,128)(2,1)S(1)} %get-tuple-element.27), channel_id=1, source_target_pairs={{0,4},{4,0},{8,12},{12,8},{16,20},{20,16},{24,28},{28,24},{32,36},... | collective-permute-start | bytes 442376 | tf_op jit(solution)/shard_map/ppermute | solution.py:132
  11.4 8.6 %collective-permute-start.1 = (bf16[192,384]{1,0:T(8,128)(2,1)S(1)}, bf16[192,384]{1,0:T(8,128)(2,1)S(1)}, u32[]{:S(2)}, u32[]{:S(2)}) collective-permute-start(bf16[192,384]{1,0:T(8,128)(2,1)S(1)} %get-tuple-element.26), channel_id=1, source_target_pairs={{0,4},{4,0},{8,12},{12,8},{16,20},{20,16},{24,28},{28,24},{32,36},... | collective-permute-start | bytes 442376 | tf_op jit(solution)/shard_map/ppermute | solution.py:132
  14.7 13.5 %collective-permute-start.6 = (bf16[192,384]{1,0:T(8,128)(2,1)S(1)}, bf16[192,384]{1,0:T(8,128)(2,1)S(1)}, u32[]{:S(2)}, u32[]{:S(2)}) collective-permute-start(bf16[192,384]{1,0:T(8,128)(2,1)S(1)} %get-tuple-element.24), channel_id=1, source_target_pairs={{0,4},{4,0},{8,12},{12,8},{16,20},{20,16},{24,28},{28,24},{32,36},... | collective-permute-start | bytes 442376 | tf_op jit(solution)/shard_map/ppermute | solution.py:132
  20.8 23.5 %collective-permute-start.2 = (bf16[384,384]{1,0:T(8,128)(2,1)}, bf16[384,384]{1,0:T(8,128)(2,1)}, u32[]{:S(2)}, u32[]{:S(2)}) collective-permute-start(bf16[384,384]{1,0:T(8,128)(2,1)} %maximum_select_fusion.4), channel_id=1, source_target_pairs={{0,8},{4,12},{8,16},{12,20},{16,24},{20,28},{24,32},{28,36},{32,40... | collective-permute-start | bytes 884744 | tf_op jit(solution)/shard_map/ppermute | solution.py:146
  26.2 21.7 %collective-permute-start.3 = (bf16[384,384]{1,0:T(8,128)(2,1)}, bf16[384,384]{1,0:T(8,128)(2,1)S(1)}, u32[]{:S(2)}, u32[]{:S(2)}) collective-permute-start(bf16[384,384]{1,0:T(8,128)(2,1)} %maximum_select_fusion.4), channel_id=1, source_target_pairs={{8,0},{12,4},{16,8},{20,12},{24,16},{28,20},{32,24},{36,28},{40,32... | collective-permute-start | bytes 884744 | tf_op jit(solution)/shard_map/ppermute | solution.py:147
  29.0 24.7 %collective-permute-start.8 = (bf16[384,384]{1,0:T(8,128)(2,1)}, bf16[384,384]{1,0:T(8,128)(2,1)S(1)}, u32[]{:S(2)}, u32[]{:S(2)}) collective-permute-start(bf16[384,384]{1,0:T(8,128)(2,1)} %maximum_select_fusion.5), channel_id=1, source_target_pairs={{8,0},{12,4},{16,8},{20,12},{24,16},{28,20},{32,24},{36,28},{40,32... | collective-permute-start | bytes 884744 | tf_op jit(solution)/shard_map/ppermute | solution.py:147
  30.9 29.2 %collective-permute-start.7 = (bf16[384,384]{1,0:T(8,128)(2,1)}, bf16[384,384]{1,0:T(8,128)(2,1)S(1)}, u32[]{:S(2)}, u32[]{:S(2)}) collective-permute-start(bf16[384,384]{1,0:T(8,128)(2,1)} %maximum_select_fusion.5), channel_id=1, source_target_pairs={{0,8},{4,12},{8,16},{12,20},{16,24},{20,28},{24,32},{28,36},{32,40... | collective-permute-start | bytes 884744 | tf_op jit(solution)/shard_map/ppermute | solution.py:146
  37.1 23.2 %collective-permute-start.4 = (bf16[192,768]{1,0:T(8,128)(2,1)}, bf16[192,768]{1,0:T(8,128)(2,1)S(1)}, u32[]{:S(2)}, u32[]{:S(2)}) collective-permute-start(bf16[192,768]{1,0:T(8,128)(2,1)} %bitcast.68), channel_id=1, source_target_pairs={{0,0},{1,32},{2,64},{3,96},{32,1},{33,33},{34,65},{35,97},{64,2},{... | collective-permute-start | bytes 884744 | tf_op jit(solution)/shard_map/ppermute | solution.py:169
  44.3 16.0 %collective-permute-start.5 = (f32[768]{0:T(1024)S(1)}, f32[768]{0:T(1024)S(1)}, u32[]{:S(2)}, u32[]{:S(2)}) collective-permute-start(f32[768]{0:T(1024)S(1)} %reduce), channel_id=1, source_target_pairs={{0,0},{1,32},{2,64},{3,96},{32,1},{33,33},{34,65},{35,97},{64,2},{... | collective-permute-start | bytes 9224 | tf_op jit(solution)/shard_map/ppermute | solution.py:170
  70.8 7.2 %collective-permute-start.9 = (bf16[192,384]{0,1:T(8,128)(2,1)S(1)}, bf16[192,384]{0,1:T(8,128)(2,1)S(1)}, u32[]{:S(2)}, u32[]{:S(2)}) collective-permute-start(bf16[192,384]{0,1:T(8,128)(2,1)S(1)} %get-tuple-element.22), channel_id=1, source_target_pairs={{0,4},{4,0},{8,12},{12,8},{16,20},{20,16},{24,28},{28,24},{32,36},... | collective-permute-start | bytes 442376 | tf_op jit(solution)/shard_map/ppermute | solution.py:194
  79.4 18.4 %copy-start = (bf16[1,768,768]{1,2,0:T(8,128)(2,1)S(1)}, bf16[1,768,768]{1,2,0:T(8,128)(2,1)}, u32[]{:S(2)}) copy-start(bf16[1,768,768]{1,2,0:T(8,128)(2,1)} %all-gather.3.cloned.1.call-done) | copy-start | bytes 3538948
  79.4 18.4 %all-to-all-start = ((bf16[4,192,768]{2,1,0:T(8,128)(2,1)}), bf16[4,192,768]{2,1,0:T(8,128)(2,1)S(1)}, u32[]{:S(2)}, u32[]{:S(2)}) async-start(bf16[4,192,768]{2,1,0:T(8,128)(2,1)} %broadcast_in_dim.31), calls=%async_computation | async-start | bytes 2359296 | tf_op jit(solution)/shard_map/all_to_all | solution.py:201
  99.1 12.5 %collective-permute-start.12 = (bf16[192,768]{1,0:T(8,128)(2,1)}, bf16[192,768]{1,0:T(8,128)(2,1)S(1)}, u32[]{:S(2)}, u32[]{:S(2)}) collective-permute-start(bf16[192,768]{1,0:T(8,128)(2,1)} %convolution_convert_fusion), channel_id=1, source_target_pairs={{0,3},{1,0},{2,1},{3,2},{4,7},{5,4},{6,5},{7,6},{8,11},{9,8},{10,9... | collective-permute-start | bytes 884744 | tf_op jit(solution)/shard_map/ppermute | solution.py:212
  102.3 23.0 %collective-permute-start.11 = (bf16[192,768]{1,0:T(8,128)(2,1)}, bf16[192,768]{1,0:T(8,128)(2,1)S(1)}, u32[]{:S(2)}, u32[]{:S(2)}) collective-permute-start(bf16[192,768]{1,0:T(8,128)(2,1)} %convolution_convert_fusion.1), channel_id=1, source_target_pairs={{0,2},{1,3},{2,0},{3,1},{4,6},{5,7},{6,4},{7,5},{8,10},{9,11},{10,... | collective-permute-start | bytes 884744 | tf_op jit(solution)/shard_map/ppermute | solution.py:212
  109.7 22.2 %collective-permute-start.10 = (bf16[192,768]{1,0:T(8,128)(2,1)}, bf16[192,768]{1,0:T(8,128)(2,1)S(1)}, u32[]{:S(2)}, u32[]{:S(2)}) collective-permute-start(bf16[192,768]{1,0:T(8,128)(2,1)} %convolution_convert_fusion.2), channel_id=1, source_target_pairs={{0,1},{1,2},{2,3},{3,0},{4,5},{5,6},{6,7},{7,4},{8,9},{9,10},{10,1... | collective-permute-start | bytes 884744 | tf_op jit(solution)/shard_map/ppermute | solution.py:212
  132.5 21.0 %collective-permute-start.13 = (bf16[192,768]{1,0:T(8,128)(2,1)S(1)}, bf16[192,768]{1,0:T(8,128)(2,1)S(1)}, u32[]{:S(2)}, u32[]{:S(2)}) collective-permute-start(bf16[192,768]{1,0:T(8,128)(2,1)S(1)} %add_convert_fusion), channel_id=1, source_target_pairs={{0,128},{1,160},{2,192},{3,224},{32,129},{33,161},{34,193},{35,225... | collective-permute-start | bytes 884744 | tf_op jit(solution)/shard_map/ppermute | solution.py:220
Sparse Core Ops, SparseCore 0:
  9.4 58.0 all-gather.2
where the time goes:
time: 162 us; the launch traced here: 161 us
  waiting for transfers between devices  80.3 us (50%)
  starting transfers between devices  46.2 us (29%)
  between operations  15.8 us (10%)
  matrix products  7.39 us (5%)
  local copies, waits for them, and re-layouts  7.23 us (4%)
  other arithmetic  4.11 us (3%)
    ppermute x3, waiting for transfers between devices, on_device(): received.append(lax.ppermute(outgoing, 'head', route))  20.2 us
    ppermute x1, waiting for transfers between devices, on_device(): handed = lax.ppermute(updated, ('section', 'sx', 'head'), hand)  17.9 us
    all_to_all x1, waiting for transfers between devices, on_device(): token_parts = lax.all_to_all(spread, 'sx', 0, 0)  14.5 us
    ppermute x2, starting transfers between devices, on_device(): lax.ppermute((tile_k, tile_v), seq, [(i, i + 2) for i in range(seq_count...  10.9 us
    ppermute x3, starting transfers between devices, on_device(): received.append(lax.ppermute(outgoing, 'head', route))  9.97 us
    ppermute x2, waiting for transfers between devices, on_device(): lax.ppermute((tile_k, tile_v), seq, [(i, i + 2) for i in range(seq_count...  9.49 us
    ppermute x3, starting transfers between devices, on_device(): lax.ppermute((partner_half(queries), partner_half(own_keys), partner_half...  7.35 us
    all_gather x1, waiting for transfers between devices, on_device(): weight_block = lax.all_gather(out_weight[0], 'sy', axis=1, tiled=True)  7.23 us
  transfers between devices with their start and end apart: 16, of which 9 were waited for; matrix products, arithmetic and copies ran while one was open for 7% of the time, Pallas kernels for 0%

commit v1 on v0

--- a/solution.py
+++ b/solution.py
@@ -163,7 +163,9 @@
     query_float = query_parts.astype(jnp.float32)
     query_lengths = jnp.sqrt(jnp.sum(query_float * query_float, axis=2))
     row_bound = query_lengths * bound[None, :] * score_scale
-    weight_block = lax.all_gather(out_weight[0], "sy", axis=1, tiled=True)
+    weight_block = jnp.concatenate(
+        lax.all_to_all(jnp.stack([out_weight[0]] * lax.axis_size("sy")), "sy", 0, 0), axis=1
+    )
     swap = linear_pairs((x_count, head_groups), lambda a, b: (b, a))
     stream_in, gate_in, _ = lax.optimization_barrier((stream[0], gate_scale[0], tile_k))
     stream_block = lax.ppermute(stream_in, ("sx", "head"), swap)

time: 162 us -> 174 us (1.074)
  the two profiles are of different devices: /device:TPU:153 before, /device:TPU:60 now
where the time goes in v1:
time: 174 us; the launch traced here: 173 us
  starting transfers between devices  75.5 us (43%)
  waiting for transfers between devices  72.2 us (41%)
  local copies, waits for them, and re-layouts  11.3 us (6%)
  matrix products  7.65 us (4%)
  other arithmetic  4.1 us (2%)
  between operations  2.36 us (1%)
    ppermute x3, waiting for transfers between devices, on_device(): lax.ppermute((partner_half(queries), partner_half(own_keys), partner_half...  21.7 us
    ppermute x3, starting transfers between devices, on_device(): received.append(lax.ppermute(outgoing, 'head', route))  19.3 us
    ppermute x1, waiting for transfers between devices, on_device(): handed = lax.ppermute(updated, ('section', 'sx', 'head'), hand)  15.9 us
    ppermute x3, waiting for transfers between devices, on_device(): received.append(lax.ppermute(outgoing, 'head', route))  14.6 us
    all_to_all x1, waiting for transfers between devices, on_device(): token_parts = lax.all_to_all(spread, 'sx', 0, 0)  10.9 us
    ppermute x3, starting transfers between devices, on_device(): lax.ppermute((partner_half(queries), partner_half(own_keys), partner_half...  9.34 us
    ppermute x2, starting transfers between devices, on_device(): lax.ppermute((tile_k, tile_v), seq, [(i, i - 2) for i in range(2, seq_cou...  8.3 us
    ppermute x2, starting transfers between devices, on_device(): lax.ppermute((tile_k, tile_v), seq, [(i, i + 2) for i in range(seq_count...  7.28 us
  transfers between devices with their start and end apart: 16, of which 8 were waited for; matrix products, arithmetic and copies ran while one was open for 8% of the time, Pallas kernels for 0%

profile of v1, /device:TPU:60, one launch (start us, length us, event | category | flops | bytes accessed | tf_op | source)
XLA Modules:
  0.0 173.1 jit_solution(15884435818713380871)
XLA Ops:
  0.0 2.0 %stack.3 = bf16[8,768,96]{1,2,0:T(8,128)(2,1)} broadcast(bf16[768,96]{0,1:T(8,128)(2,1)} %bitcast.71), dimensions={1,2} | broadcast | bytes 1327104 | tf_op jit(solution)/shard_map/stack | solution.py:167
  2.0 7.0 %all-to-all-start = ((bf16[8,768,96]{1,2,0:T(8,128)(2,1)}), bf16[8,768,96]{1,2,0:T(8,128)(2,1)S(1)}, u32[]{:S(2)}, u32[]{:S(2)}) async-start(bf16[8,768,96]{1,2,0:T(8,128)(2,1)} %stack.3), calls=%async_computation | async-start | bytes 2359296 | tf_op jit(solution)/shard_map/all_to_all | solution.py:167
  9.1 3.5 %collective-permute-start = (bf16[192,384]{1,0:T(8,128)(2,1)S(1)}, bf16[192,384]{1,0:T(8,128)(2,1)S(1)}, u32[]{:S(2)}, u32[]{:S(2)}) collective-permute-start(bf16[192,384]{1,0:T(8,128)(2,1)S(1)} %get-tuple-element.27), channel_id=1, source_target_pairs={{0,4},{4,0},{8,12},{12,8},{16,20},{20,16},{24,28},{28,24},{32,36},... | collective-permute-start | bytes 442376 | tf_op jit(solution)/shard_map/ppermute | solution.py:132
  12.7 2.5 %collective-permute-start.1 = (bf16[192,384]{1,0:T(8,128)(2,1)S(1)}, bf16[192,384]{1,0:T(8,128)(2,1)S(1)}, u32[]{:S(2)}, u32[]{:S(2)}) collective-permute-start(bf16[192,384]{1,0:T(8,128)(2,1)S(1)} %get-tuple-element.26), channel_id=1, source_target_pairs={{0,4},{4,0},{8,12},{12,8},{16,20},{20,16},{24,28},{28,24},{32,36},... | collective-permute-start | bytes 442376 | tf_op jit(solution)/shard_map/ppermute | solution.py:132
  15.2 3.4 %collective-permute-start.6 = (bf16[192,384]{1,0:T(8,128)(2,1)S(1)}, bf16[192,384]{1,0:T(8,128)(2,1)S(1)}, u32[]{:S(2)}, u32[]{:S(2)}) collective-permute-start(bf16[192,384]{1,0:T(8,128)(2,1)S(1)} %get-tuple-element.24), channel_id=1, source_target_pairs={{0,4},{4,0},{8,12},{12,8},{16,20},{20,16},{24,28},{28,24},{32,36},... | collective-permute-start | bytes 442376 | tf_op jit(solution)/shard_map/ppermute | solution.py:132
  21.8 21.7 %collective-permute-done.1 = bf16[192,384]{1,0:T(8,128)(2,1)S(1)} collective-permute-done((bf16[192,384]{1,0:T(8,128)(2,1)S(1)}, bf16[192,384]{1,0:T(8,128)(2,1)S(1)}, u32[]{:S(2)}, u32[]{:S(2)}) %collective-permute-start.1) | collective-permute-done | bytes 147488 | tf_op jit(solution)/shard_map/ppermute | solution.py:132
  44.3 2.9 %collective-permute-start.2 = (bf16[384,384]{1,0:T(8,128)(2,1)}, bf16[384,384]{1,0:T(8,128)(2,1)}, u32[]{:S(2)}, u32[]{:S(2)}) collective-permute-start(bf16[384,384]{1,0:T(8,128)(2,1)} %maximum_select_fusion.4), channel_id=1, source_target_pairs={{0,8},{4,12},{8,16},{12,20},{16,24},{20,28},{24,32},{28,36},{32,40... | collective-permute-start | bytes 884744 | tf_op jit(solution)/shard_map/ppermute | solution.py:146
  47.2 3.8 %collective-permute-start.3 = (bf16[384,384]{1,0:T(8,128)(2,1)}, bf16[384,384]{1,0:T(8,128)(2,1)}, u32[]{:S(2)}, u32[]{:S(2)}) collective-permute-start(bf16[384,384]{1,0:T(8,128)(2,1)} %maximum_select_fusion.4), channel_id=1, source_target_pairs={{8,0},{12,4},{16,8},{20,12},{24,16},{28,20},{32,24},{36,28},{40,32... | collective-permute-start | bytes 884744 | tf_op jit(solution)/shard_map/ppermute | solution.py:147
  51.0 0.8 maximum_select_fusion.5
  51.8 4.5 %collective-permute-start.8 = (bf16[384,384]{1,0:T(8,128)(2,1)}, bf16[384,384]{1,0:T(8,128)(2,1)}, u32[]{:S(2)}, u32[]{:S(2)}) collective-permute-start(bf16[384,384]{1,0:T(8,128)(2,1)} %maximum_select_fusion.5), channel_id=1, source_target_pairs={{8,0},{12,4},{16,8},{20,12},{24,16},{28,20},{32,24},{36,28},{40,32... | collective-permute-start | bytes 884744 | tf_op jit(solution)/shard_map/ppermute | solution.py:147
  56.4 4.3 %collective-permute-start.7 = (bf16[384,384]{1,0:T(8,128)(2,1)}, bf16[384,384]{1,0:T(8,128)(2,1)}, u32[]{:S(2)}, u32[]{:S(2)}) collective-permute-start(bf16[384,384]{1,0:T(8,128)(2,1)} %maximum_select_fusion.5), channel_id=1, source_target_pairs={{0,8},{4,12},{8,16},{12,20},{16,24},{20,28},{24,32},{28,36},{32,40... | collective-permute-start | bytes 884744 | tf_op jit(solution)/shard_map/ppermute | solution.py:146
  61.5 6.0 %collective-permute-start.4 = (bf16[192,768]{1,0:T(8,128)(2,1)}, bf16[192,768]{1,0:T(8,128)(2,1)}, u32[]{:S(2)}, u32[]{:S(2)}) collective-permute-start(bf16[192,768]{1,0:T(8,128)(2,1)} %bitcast.72), channel_id=1, source_target_pairs={{0,0},{1,32},{2,64},{3,96},{32,1},{33,33},{34,65},{35,97},{64,2},{... | collective-permute-start | bytes 884744 | tf_op jit(solution)/shard_map/ppermute | solution.py:171
  68.5 3.1 %collective-permute-start.5 = (f32[768]{0:T(1024)S(1)}, f32[768]{0:T(1024)S(1)}, u32[]{:S(2)}, u32[]{:S(2)}) collective-permute-start(f32[768]{0:T(1024)S(1)} %reduce), channel_id=1, source_target_pairs={{0,0},{1,32},{2,64},{3,96},{32,1},{33,33},{34,65},{35,97},{64,2},{... | collective-permute-start | bytes 9224 | tf_op jit(solution)/shard_map/ppermute | solution.py:172
  71.7 1.2 copy.78
  73.2 1.2 copy.80
  74.9 3.1 %collective-permute-done.8 = bf16[384,384]{1,0:T(8,128)(2,1)} collective-permute-done((bf16[384,384]{1,0:T(8,128)(2,1)}, bf16[384,384]{1,0:T(8,128)(2,1)}, u32[]{:S(2)}, u32[]{:S(2)}) %collective-permute-start.8) | collective-permute-done | bytes 294944 | tf_op jit(solution)/shard_map/ppermute | solution.py:147
  78.0 1.2 copy.90
  79.2 1.8 %copy.81 = bf16[384,384]{0,1:T(8,128)(2,1)} copy(bf16[384,384]{1,0:T(8,128)(2,1)} %collective-permute-done.7) | data formatting | bytes 589824 | tf_op jit(solution)/shard_map/ppermute | solution.py:146
  84.9 1.9 %collective-permute-start.9 = (bf16[192,384]{0,1:T(8,128)(2,1)S(1)}, bf16[192,384]{0,1:T(8,128)(2,1)S(1)}, u32[]{:S(2)}, u32[]{:S(2)}) collective-permute-start(bf16[192,384]{0,1:T(8,128)(2,1)S(1)} %get-tuple-element.22), channel_id=1, source_target_pairs={{0,4},{4,0},{8,12},{12,8},{16,20},{20,16},{24,28},{28,24},{32,36},... | collective-permute-start | bytes 442376 | tf_op jit(solution)/shard_map/ppermute | solution.py:196
  86.8 5.6 %collective-permute-done.9 = bf16[192,384]{0,1:T(8,128)(2,1)S(1)} collective-permute-done((bf16[192,384]{0,1:T(8,128)(2,1)S(1)}, bf16[192,384]{0,1:T(8,128)(2,1)S(1)}, u32[]{:S(2)}, u32[]{:S(2)}) %collective-permute-start.9) | collective-permute-done | bytes 147488 | tf_op jit(solution)/shard_map/ppermute | solution.py:196
  92.7 1.1 broadcast_in_dim.31
  93.8 6.1 %all-to-all-start.1 = ((bf16[4,192,768]{2,1,0:T(8,128)(2,1)}), bf16[4,192,768]{2,1,0:T(8,128)(2,1)S(1)}, u32[]{:S(2)}, u32[]{:S(2)}) async-start(bf16[4,192,768]{2,1,0:T(8,128)(2,1)} %broadcast_in_dim.31), calls=%async_computation.1 | async-start | bytes 2359296 | tf_op jit(solution)/shard_map/all_to_all | solution.py:203
  100.0 10.9 %all-to-all-done.1 = bf16[4,192,768]{2,1,0:T(8,128)(2,1)S(1)} async-done(((bf16[4,192,768]{2,1,0:T(8,128)(2,1)}), bf16[4,192,768]{2,1,0:T(8,128)(2,1)S(1)}, u32[]{:S(2)}, u32[]{:S(2)}) %all-to-all-start.1) | async-done | bytes 1179680 | tf_op jit(solution)/shard_map/all_to_all | solution.py:203
  111.4 15.0 %collective-permute-start.12 = (bf16[192,768]{1,0:T(8,128)(2,1)S(1)}, bf16[192,768]{1,0:T(8,128)(2,1)S(1)}, u32[]{:S(2)}, u32[]{:S(2)}) collective-permute-start(bf16[192,768]{1,0:T(8,128)(2,1)S(1)} %convolution_convert_fusion), channel_id=1, source_target_pairs={{0,3},{1,0},{2,1},{3,2},{4,7},{5,4},{6,5},{7,6},{8,11},{9,8},{10,9... | collective-permute-start | bytes 884744 | tf_op jit(solution)/shard_map/ppermute | solution.py:214
  126.4 1.3 convolution_convert_fusion.1
  127.6 1.9 %collective-permute-start.11 = (bf16[192,768]{1,0:T(8,128)(2,1)}, bf16[192,768]{1,0:T(8,128)(2,1)S(1)}, u32[]{:S(2)}, u32[]{:S(2)}) collective-permute-start(bf16[192,768]{1,0:T(8,128)(2,1)} %convolution_convert_fusion.1), channel_id=1, source_target_pairs={{0,2},{1,3},{2,0},{3,1},{4,6},{5,7},{6,4},{7,5},{8,10},{9,11},{10,... | collective-permute-start | bytes 884744 | tf_op jit(solution)/shard_map/ppermute | solution.py:214
  129.5 1.3 convolution_convert_fusion.2
  130.8 2.5 %collective-permute-start.10 = (bf16[192,768]{1,0:T(8,128)(2,1)}, bf16[192,768]{1,0:T(8,128)(2,1)S(1)}, u32[]{:S(2)}, u32[]{:S(2)}) collective-permute-start(bf16[192,768]{1,0:T(8,128)(2,1)} %convolution_convert_fusion.2), channel_id=1, source_target_pairs={{0,1},{1,2},{2,3},{3,0},{4,5},{5,6},{6,7},{7,4},{8,9},{9,10},{10,1... | collective-permute-start | bytes 884744 | tf_op jit(solution)/shard_map/ppermute | solution.py:214
  133.8 14.1 %collective-permute-done.11 = bf16[192,768]{1,0:T(8,128)(2,1)S(1)} collective-permute-done((bf16[192,768]{1,0:T(8,128)(2,1)}, bf16[192,768]{1,0:T(8,128)(2,1)S(1)}, u32[]{:S(2)}, u32[]{:S(2)}) %collective-permute-start.11) | collective-permute-done | bytes 294944 | tf_op jit(solution)/shard_map/ppermute | solution.py:214
  147.9 1.6 add_convert_fusion
  149.5 7.0 %collective-permute-start.13 = (bf16[192,768]{1,0:T(8,128)(2,1)S(1)}, bf16[192,768]{1,0:T(8,128)(2,1)S(1)}, u32[]{:S(2)}, u32[]{:S(2)}) collective-permute-start(bf16[192,768]{1,0:T(8,128)(2,1)S(1)} %add_convert_fusion), channel_id=1, source_target_pairs={{0,128},{1,160},{2,192},{3,224},{32,129},{33,161},{34,193},{35,225... | collective-permute-start | bytes 884744 | tf_op jit(solution)/shard_map/ppermute | solution.py:222
  156.5 15.9 %collective-permute-done.13 = bf16[192,768]{1,0:T(8,128)(2,1)S(1)} collective-permute-done((bf16[192,768]{1,0:T(8,128)(2,1)S(1)}, bf16[192,768]{1,0:T(8,128)(2,1)S(1)}, u32[]{:S(2)}, u32[]{:S(2)}) %collective-permute-start.13) | collective-permute-done | bytes 294944 | tf_op jit(solution)/shard_map/ppermute | solution.py:222
  (58 shorter events, 10.6 us)
Async XLA Ops:
  2.0 7.0 %copy-start = (bf16[1,192,768]{2,1,0:T(8,128)(2,1)S(1)}, bf16[1,192,768]{2,1,0:T(8,128)(2,1)}, u32[]{:S(2)}) copy-start(bf16[1,192,768]{2,1,0:T(8,128)(2,1)} %param.7) | copy-start | bytes 884740
  2.0 10.6 %copy-start.1 = (bf16[1,192,768]{2,1,0:T(8,128)(2,1)S(1)}, bf16[1,192,768]{2,1,0:T(8,128)(2,1)}, u32[]{:S(2)}) copy-start(bf16[1,192,768]{2,1,0:T(8,128)(2,1)} %param.8) | copy-start | bytes 884740
  2.0 79.0 %all-to-all-start = ((bf16[8,768,96]{1,2,0:T(8,128)(2,1)}), bf16[8,768,96]{1,2,0:T(8,128)(2,1)S(1)}, u32[]{:S(2)}, u32[]{:S(2)}) async-start(bf16[8,768,96]{1,2,0:T(8,128)(2,1)} %stack.3), calls=%async_computation | async-start | bytes 2359296 | tf_op jit(solution)/shard_map/all_to_all | solution.py:167
  9.0 6.1 %copy-start.2 = (bf16[1,192,768]{2,1,0:T(8,128)(2,1)S(1)}, bf16[1,192,768]{2,1,0:T(8,128)(2,1)}, u32[]{:S(2)}) copy-start(bf16[1,192,768]{2,1,0:T(8,128)(2,1)} %param.9) | copy-start | bytes 884740
  9.0 9.6 %copy-start.4 = (s32[16,27]{1,0:T(8,128)S(1)}, s32[16,27]{1,0:T(8,128)}, u32[]{:S(2)}) copy-start(s32[16,27]{1,0:T(8,128)} %param.13) | copy-start | bytes 5188
  9.1 12.7 %copy-start.5 = (f32[1,768]{1,0:T(1,128)S(1)}, f32[1,768]{1,0:T(1,128)}, u32[]{:S(2)}) copy-start(f32[1,768]{1,0:T(1,128)} %param.12) | copy-start | bytes 9220
  9.1 52.4 %collective-permute-start = (bf16[192,384]{1,0:T(8,128)(2,1)S(1)}, bf16[192,384]{1,0:T(8,128)(2,1)S(1)}, u32[]{:S(2)}, u32[]{:S(2)}) collective-permute-start(bf16[192,384]{1,0:T(8,128)(2,1)S(1)} %get-tuple-element.27), channel_id=1, source_target_pairs={{0,4},{4,0},{8,12},{12,8},{16,20},{20,16},{24,28},{28,24},{32,36},... | collective-permute-start | bytes 442376 | tf_op jit(solution)/shard_map/ppermute | solution.py:132
  12.7 30.8 %collective-permute-start.1 = (bf16[192,384]{1,0:T(8,128)(2,1)S(1)}, bf16[192,384]{1,0:T(8,128)(2,1)S(1)}, u32[]{:S(2)}, u32[]{:S(2)}) collective-permute-start(bf16[192,384]{1,0:T(8,128)(2,1)S(1)} %get-tuple-element.26), channel_id=1, source_target_pairs={{0,4},{4,0},{8,12},{12,8},{16,20},{20,16},{24,28},{28,24},{32,36},... | collective-permute-start | bytes 442376 | tf_op jit(solution)/shard_map/ppermute | solution.py:132
  15.2 35.9 %collective-permute-start.6 = (bf16[192,384]{1,0:T(8,128)(2,1)S(1)}, bf16[192,384]{1,0:T(8,128)(2,1)S(1)}, u32[]{:S(2)}, u32[]{:S(2)}) collective-permute-start(bf16[192,384]{1,0:T(8,128)(2,1)S(1)} %get-tuple-element.24), channel_id=1, source_target_pairs={{0,4},{4,0},{8,12},{12,8},{16,20},{20,16},{24,28},{28,24},{32,36},... | collective-permute-start | bytes 442376 | tf_op jit(solution)/shard_map/ppermute | solution.py:132
  44.3 24.2 %collective-permute-start.2 = (bf16[384,384]{1,0:T(8,128)(2,1)}, bf16[384,384]{1,0:T(8,128)(2,1)}, u32[]{:S(2)}, u32[]{:S(2)}) collective-permute-start(bf16[384,384]{1,0:T(8,128)(2,1)} %maximum_select_fusion.4), channel_id=1, source_target_pairs={{0,8},{4,12},{8,16},{12,20},{16,24},{20,28},{24,32},{28,36},{32,40... | collective-permute-start | bytes 884744 | tf_op jit(solution)/shard_map/ppermute | solution.py:146
  47.2 25.9 %collective-permute-start.3 = (bf16[384,384]{1,0:T(8,128)(2,1)}, bf16[384,384]{1,0:T(8,128)(2,1)}, u32[]{:S(2)}, u32[]{:S(2)}) collective-permute-start(bf16[384,384]{1,0:T(8,128)(2,1)} %maximum_select_fusion.4), channel_id=1, source_target_pairs={{8,0},{12,4},{16,8},{20,12},{24,16},{28,20},{32,24},{36,28},{40,32... | collective-permute-start | bytes 884744 | tf_op jit(solution)/shard_map/ppermute | solution.py:147
  51.8 26.2 %collective-permute-start.8 = (bf16[384,384]{1,0:T(8,128)(2,1)}, bf16[384,384]{1,0:T(8,128)(2,1)}, u32[]{:S(2)}, u32[]{:S(2)}) collective-permute-start(bf16[384,384]{1,0:T(8,128)(2,1)} %maximum_select_fusion.5), channel_id=1, source_target_pairs={{8,0},{12,4},{16,8},{20,12},{24,16},{28,20},{32,24},{36,28},{40,32... | collective-permute-start | bytes 884744 | tf_op jit(solution)/shard_map/ppermute | solution.py:147
  56.4 22.8 %collective-permute-start.7 = (bf16[384,384]{1,0:T(8,128)(2,1)}, bf16[384,384]{1,0:T(8,128)(2,1)}, u32[]{:S(2)}, u32[]{:S(2)}) collective-permute-start(bf16[384,384]{1,0:T(8,128)(2,1)} %maximum_select_fusion.5), channel_id=1, source_target_pairs={{0,8},{4,12},{8,16},{12,20},{16,24},{20,28},{24,32},{28,36},{32,40... | collective-permute-start | bytes 884744 | tf_op jit(solution)/shard_map/ppermute | solution.py:146
  61.5 19.6 %collective-permute-start.4 = (bf16[192,768]{1,0:T(8,128)(2,1)}, bf16[192,768]{1,0:T(8,128)(2,1)}, u32[]{:S(2)}, u32[]{:S(2)}) collective-permute-start(bf16[192,768]{1,0:T(8,128)(2,1)} %bitcast.72), channel_id=1, source_target_pairs={{0,0},{1,32},{2,64},{3,96},{32,1},{33,33},{34,65},{35,97},{64,2},{... | collective-permute-start | bytes 884744 | tf_op jit(solution)/shard_map/ppermute | solution.py:171
  68.5 12.5 %collective-permute-start.5 = (f32[768]{0:T(1024)S(1)}, f32[768]{0:T(1024)S(1)}, u32[]{:S(2)}, u32[]{:S(2)}) collective-permute-start(f32[768]{0:T(1024)S(1)} %reduce), channel_id=1, source_target_pairs={{0,0},{1,32},{2,64},{3,96},{32,1},{33,33},{34,65},{35,97},{64,2},{... | collective-permute-start | bytes 9224 | tf_op jit(solution)/shard_map/ppermute | solution.py:172
  83.4 1.0 copy-start.3
  84.9 7.6 %collective-permute-start.9 = (bf16[192,384]{0,1:T(8,128)(2,1)S(1)}, bf16[192,384]{0,1:T(8,128)(2,1)S(1)}, u32[]{:S(2)}, u32[]{:S(2)}) collective-permute-start(bf16[192,384]{0,1:T(8,128)(2,1)S(1)} %get-tuple-element.22), channel_id=1, source_target_pairs={{0,4},{4,0},{8,12},{12,8},{16,20},{20,16},{24,28},{28,24},{32,36},... | collective-permute-start | bytes 442376 | tf_op jit(solution)/shard_map/ppermute | solution.py:196
  93.8 17.0 %all-to-all-start.1 = ((bf16[4,192,768]{2,1,0:T(8,128)(2,1)}), bf16[4,192,768]{2,1,0:T(8,128)(2,1)S(1)}, u32[]{:S(2)}, u32[]{:S(2)}) async-start(bf16[4,192,768]{2,1,0:T(8,128)(2,1)} %broadcast_in_dim.31), calls=%async_computation.1 | async-start | bytes 2359296 | tf_op jit(solution)/shard_map/all_to_all | solution.py:203
  111.4 22.4 %collective-permute-start.12 = (bf16[192,768]{1,0:T(8,128)(2,1)S(1)}, bf16[192,768]{1,0:T(8,128)(2,1)S(1)}, u32[]{:S(2)}, u32[]{:S(2)}) collective-permute-start(bf16[192,768]{1,0:T(8,128)(2,1)S(1)} %convolution_convert_fusion), channel_id=1, source_target_pairs={{0,3},{1,0},{2,1},{3,2},{4,7},{5,4},{6,5},{7,6},{8,11},{9,8},{10,9... | collective-permute-start | bytes 884744 | tf_op jit(solution)/shard_map/ppermute | solution.py:214
  127.6 20.3 %collective-permute-start.11 = (bf16[192,768]{1,0:T(8,128)(2,1)}, bf16[192,768]{1,0:T(8,128)(2,1)S(1)}, u32[]{:S(2)}, u32[]{:S(2)}) collective-permute-start(bf16[192,768]{1,0:T(8,128)(2,1)} %convolution_convert_fusion.1), channel_id=1, source_target_pairs={{0,2},{1,3},{2,0},{3,1},{4,6},{5,7},{6,4},{7,5},{8,10},{9,11},{10,... | collective-permute-start | bytes 884744 | tf_op jit(solution)/shard_map/ppermute | solution.py:214
  130.8 17.1 %collective-permute-start.10 = (bf16[192,768]{1,0:T(8,128)(2,1)}, bf16[192,768]{1,0:T(8,128)(2,1)S(1)}, u32[]{:S(2)}, u32[]{:S(2)}) collective-permute-start(bf16[192,768]{1,0:T(8,128)(2,1)} %convolution_convert_fusion.2), channel_id=1, source_target_pairs={{0,1},{1,2},{2,3},{3,0},{4,5},{5,6},{6,7},{7,4},{8,9},{9,10},{10,1... | collective-permute-start | bytes 884744 | tf_op jit(solution)/shard_map/ppermute | solution.py:214
  149.5 22.9 %collective-permute-start.13 = (bf16[192,768]{1,0:T(8,128)(2,1)S(1)}, bf16[192,768]{1,0:T(8,128)(2,1)S(1)}, u32[]{:S(2)}, u32[]{:S(2)}) collective-permute-start(bf16[192,768]{1,0:T(8,128)(2,1)S(1)} %add_convert_fusion), channel_id=1, source_target_pairs={{0,128},{1,160},{2,192},{3,224},{32,129},{33,161},{34,193},{35,225... | collective-permute-start | bytes 884744 | tf_op jit(solution)/shard_map/ppermute | solution.py:222
